TPU v7x, 256 devices: a whole 4x4x8 slice. The times are simulated.
256 devices in a mesh: dp: 16 (over z, core), expert: 16 (over x, y).
Axes of the slice: x: 4, y: 4, z: 8, core: 2. Of those that a mesh axis runs over, the one named last changes fastest.
Arguments:
- hidden_in: bfloat16 [16384, 2048], P(('dp', 'expert')), parts along dimension 0, may hold values from -6 to 6
- route_ids: int32 [16384, 8], P(('dp', 'expert')), parts along dimension 0, may hold values from 0 to 15, all different within a row; in each aligned block of 64 rows (0 to 63, 64 to 127, ...) at most 64 rows name the same one
- gates: float32 [16384, 8], P(('dp', 'expert')), parts along dimension 0, may hold values from 0.05 to 1
- w_in: bfloat16 [16, 2048, 1536], P('expert'), may hold values from -0.125 to 0.125
- w_out: bfloat16 [16, 768, 2048], P('expert'), may hold values from -0.21875 to 0.21875
Outputs:
- combined: bfloat16 [16384, 2048], P(('dp', 'expert')), parts along dimension 0
There are 16 independent parts, one for each index of `dp`. A program takes and returns all parts, laid end to end along the dimension named above; an argument that names none is the same for every part. Nothing has to cross between parts.
Inputs may be any that keep to these rules, and one draw needn't show every extreme that they name: `route_ids`: each row names 8 different experts. Among the rows of one device (aligned blocks of 64 rows) no expert is named by more than 64 rows, and in every draw some expert is named by exactly 64 rows of some block.
All inputs are finite; a program needn't handle non-finite values.
Results may differ from a plain program's by a relative error of at most 0.0085.
Values may be sent and summed in bfloat16 or wider, within the bound.
No kernel may reach another device: no remote copies, remote signals or barrier semaphores. Data moves between devices by JAX's collectives and lax.ppermute only.
A program may use at most 64 MiB of HBM per device.

v0:
```python
import jax
import jax.numpy as jnp
from jax import lax
from jax.sharding import PartitionSpec as P


def slot_ranks(choices, count):
    flat = choices.reshape(choices.shape[:-2] + (-1,))
    length = flat.shape[-1]
    onehot = (flat[..., None] == jnp.arange(count, dtype=jnp.int32)).astype(jnp.bfloat16)
    lower = (
        jnp.arange(length, dtype=jnp.int32)[:, None] > jnp.arange(length, dtype=jnp.int32)[None, :]
    ).astype(jnp.bfloat16)
    ranks = jnp.einsum("ij,...jn->...in", lower, onehot, preferred_element_type=jnp.float32)
    picked = jnp.sum(ranks * onehot.astype(jnp.float32), axis=-1)
    return picked.astype(jnp.int32).reshape(choices.shape)


def body(hidden_in, route_ids, gates, w_in, w_out):
    groups = lax.axis_size("expert")
    rows_here = hidden_in.shape[0]
    capacity = 2 * rows_here * route_ids.shape[1] // groups
    width = hidden_in.shape[1]
    half = w_out.shape[1]
    slots_all = capacity * groups
    slot_of = slot_ranks(route_ids, groups)
    place_key = slot_of * groups + route_ids
    key_table = (place_key[:, :, None] == jnp.arange(slots_all, dtype=jnp.int32)).astype(
        jnp.float32
    )
    placement = jnp.sum(key_table, axis=1).astype(jnp.bfloat16)
    outgoing = jnp.einsum("rs,rd->sd", placement, hidden_in, preferred_element_type=jnp.float32)
    outgoing = outgoing.astype(jnp.bfloat16).reshape(capacity, groups, width)
    projected = jnp.einsum(
        "cnd,df->cnf",
        lax.all_to_all(outgoing, "expert", split_axis=1, concat_axis=1, tiled=True),
        w_in[0],
        preferred_element_type=jnp.float32,
    )
    inner = (jax.nn.silu(projected[..., :half]) * projected[..., half:]).astype(jnp.bfloat16)
    produced = jnp.einsum(
        "cnf,fd->cnd", inner, w_out[0], preferred_element_type=jnp.float32
    ).astype(jnp.bfloat16)
    returned = lax.all_to_all(produced, "expert", split_axis=1, concat_axis=1, tiled=True)
    weighting = jnp.sum(gates[:, :, None] * key_table, axis=1)
    total = jnp.dot(
        weighting,
        returned.reshape(slots_all, width).astype(jnp.float32),
        precision=lax.Precision.HIGHEST,
    )
    return total.astype(jnp.bfloat16)


def solution(mesh):
    placed = (
        P(("dp", "expert"), None),
        P(("dp", "expert"), None),
        P(("dp", "expert"), None),
        P("expert", None, None),
        P("expert", None, None),
    )
    return jax.shard_map(
        body, mesh=mesh, in_specs=placed, out_specs=P(("dp", "expert"), None), check_vma=False
    )
```

profile of v0, /device:TPU:64, one launch (start us, length us, event | category | flops | bytes accessed | tf_op | source)
XLA Modules:
  0.0 137.9 jit_solution(10188751769058922130)
XLA Ops:
  0.0 0.0 copy-start
  0.0 0.9 copy.24
  0.9 0.1 eq.28
  1.0 0.3 fusion.7
  1.3 0.1 mul.30
  1.4 0.8 copy.26
  2.2 1.3 convert_reduce_fusion
  3.5 2.2 %convolution_convert_fusion.1 = bf16[1024,2048]{1,0:T(8,128)(2,1)S(1)} fusion(bf16[64,2048]{1,0:T(8,128)(2,1)} %param.5, bf16[64,1024]{1,0:T(8,128)(2,1)S(1)} %get-tuple-element.5), kind=kOutput, calls=%fused_computation.4 | convolution fusion | flops 270532608 | bytes 4587520 | tf_op jit(solution)/shard_map/rs,rd->sd/dot_general | solution.py:32
  5.8 0.0 slice-start
  5.8 2.3 %copy.27 = bf16[64,16,2048]{2,0,1:T(8,128)(2,1)S(1)} copy(bf16[64,16,2048]{2,1,0:T(8,128)(2,1)S(1)} %bitcast.15) | data formatting | bytes 8388608 | tf_op jit(solution)/shard_map/reshape | solution.py:33
  8.1 0.0 slice-start.1
  8.1 57.7 %all_to_all.10 = bf16[64,16,2048]{2,0,1:T(8,128)(2,1)S(1)} all-to-all(bf16[64,16,2048]{2,0,1:T(8,128)(2,1)S(1)} %copy.27), channel_id=1, replica_groups=mesh['dp'=16,'expert'=16] {'expert'}, dimensions={1} | all-to-all | bytes 8388608 | tf_op jit(solution)/shard_map/all_to_all | solution.py:36
  65.8 0.0 slice-done
  65.8 0.0 slice-done.1
  65.8 7.1 %fusion = f32[64,16,1536]{2,1,0:T(8,128)S(1)} fusion(bf16[1,2048,1536]{2,1,0:T(8,128)(2,1)S(1)} %bitcast.17, bf16[64,16,2048]{2,0,1:T(8,128)(2,1)S(1)} %all_to_all.10), kind=kOutput, calls=%fused_computation | convolution fusion | flops 6442450944 | bytes 16777216 | tf_op jit(solution)/shard_map/cnd,df->cnf/dot_general | solution.py:34
  72.9 0.0 copy-done
  72.9 3.7 %convolution_convert_fusion = bf16[64,16,2048]{2,1,0:T(8,128)(2,1)S(1)} fusion(bf16[1,768,2048]{2,1,0:T(8,128)(2,1)S(1)} %copy-done, f32[64,16,1536]{2,1,0:T(8,128)S(1)} %fusion), kind=kOutput, calls=%fused_computation.3 | convolution fusion | flops 3228041216 | bytes 13631488 | tf_op jit(solution)/shard_map/cnf,fd->cnd/dot_general | solution.py:41
  76.6 2.3 %copy.29 = bf16[64,16,2048]{2,0,1:T(8,128)(2,1)S(1)} copy(bf16[64,16,2048]{2,1,0:T(8,128)(2,1)S(1)} %convolution_convert_fusion) | data formatting | bytes 8388608 | tf_op jit(solution)/shard_map/convert_element_type | solution.py:43
  79.0 53.7 %all_to_all.11 = bf16[64,16,2048]{2,0,1:T(8,128)(2,1)S(1)} all-to-all(bf16[64,16,2048]{2,0,1:T(8,128)(2,1)S(1)} %copy.29), channel_id=1, replica_groups=mesh['dp'=16,'expert'=16] {'expert'}, dimensions={1} | all-to-all | bytes 8388608 | tf_op jit(solution)/shard_map/all_to_all | solution.py:44
  132.6 2.3 %copy.30 = bf16[64,16,2048]{2,1,0:T(8,128)(2,1)S(1)} copy(bf16[64,16,2048]{2,0,1:T(8,128)(2,1)S(1)} %all_to_all.11) | data formatting | bytes 8388608 | tf_op jit(solution)/shard_map/all_to_all | solution.py:44
  134.9 3.0 %convolution_convert_fusion.2 = bf16[64,2048]{1,0:T(8,128)(2,1)} fusion(f32[64,1024]{1,0:T(8,128)S(1)} %get-tuple-element.6, bf16[1024,2048]{1,0:T(8,128)(2,1)S(1)} %bitcast.14), kind=kOutput, calls=%fused_computation.8 | convolution fusion | flops 1610743808 | bytes 4718592 | tf_op jit(solution)/shard_map/dot_general | solution.py:46
  (3 shorter events, 0.0 us)
Async XLA Ops:
  0.0 72.9 %copy-start = (bf16[1,768,2048]{2,1,0:T(8,128)(2,1)S(1)}, bf16[1,768,2048]{2,1,0:T(8,128)(2,1)}, u32[]{:S(2)}) copy-start(bf16[1,768,2048]{2,1,0:T(8,128)(2,1)} %param.9) | copy-start | bytes 9437188
  5.8 60.0 %slice-start = ((s8[6291456]{0:T(1024)(128)(4,1)}), s8[4194304]{0:T(1024)(128)(4,1)S(1)}, s32[]{:S(2)}) async-start(s8[6291456]{0:T(1024)(128)(4,1)} %bitcast.16), calls=%async_computation.2 | async-start | bytes 8388608
  8.1 57.7 %slice-start.1 = ((s8[6291456]{0:T(1024)(128)(4,1)}), s8[2097152]{0:T(1024)(128)(4,1)S(1)}, s32[]{:S(2)}) async-start(s8[6291456]{0:T(1024)(128)(4,1)} %bitcast.16), calls=%async_computation.3 | async-start | bytes 4194304
where the time goes:
time: 138 us
  blocking collectives  111 us (80%)
  matrix products  16.3 us (12%)
  local copies, waits for them, and re-layouts  8.78 us (6%)
    all_to_all x1, blocking collectives, body(): lax.all_to_all(outgoing, 'expert', split_axis=1, concat_axis=1, tiled=True)  57.7 us
    all_to_all x1, blocking collectives, body(): lax.all_to_all(produced, 'expert', split_axis=1, concat_axis=1, tiled=True)  53.7 us
    dot_general x1, matrix products, body(): jnp.einsum('cnd,df->cnf', lax.all_to_all(outgoing, 'expert', split_axis=1...  7.13 us
    dot_general x1, matrix products, body(): jnp.einsum('cnf,fd->cnd', inner, w_out[0], preferred_element_type=jnp.flo...  3.7 us
    dot_general x1, matrix products, body(): jnp.dot(weighting, returned.reshape(slots_all, width).astype(jnp.float32)...  3.01 us

commit v1 on v0

v1 whole, which is shorter than its diff:
```python
import jax
import jax.numpy as jnp
from jax import lax
from jax.sharding import PartitionSpec as P


def body(hidden_in, route_ids, gates, w_in, w_out):
    groups = lax.axis_size("expert")
    me = lax.axis_index("expert")
    half = w_out.shape[1]
    experts = jnp.arange(groups, dtype=jnp.int32)
    dense = jnp.sum(
        jnp.where(route_ids[:, :, None] == experts, gates[:, :, None], jnp.float32(0.0)), axis=1
    )
    rows = lax.all_gather(hidden_in, "expert", axis=0, tiled=True)
    weights = lax.all_gather(dense, "expert", axis=0, tiled=True)
    mine = jnp.sum(jnp.where(experts[None, :] == me, weights, jnp.float32(0.0)), axis=1)
    projected = jnp.dot(rows, w_in[0], preferred_element_type=jnp.float32)
    inner = (jax.nn.silu(projected[:, :half]) * projected[:, half:]).astype(jnp.bfloat16)
    produced = jnp.dot(inner, w_out[0], preferred_element_type=jnp.float32).astype(jnp.bfloat16)
    weighted = (mine[:, None] * produced.astype(jnp.float32)).astype(jnp.bfloat16)
    total = lax.psum_scatter(weighted, "expert", scatter_dimension=0, tiled=True)
    return total


def solution(mesh):
    placed = (
        P(("dp", "expert"), None),
        P(("dp", "expert"), None),
        P(("dp", "expert"), None),
        P("expert", None, None),
        P("expert", None, None),
    )
    return jax.shard_map(
        body, mesh=mesh, in_specs=placed, out_specs=P(("dp", "expert"), None), check_vma=False
    )
```

time: 138 us -> 174 us (1.26)
  waiting for transfers between devices: 0 us -> 120 us
  blocking collectives: 111 us -> 24.1 us
  between operations: 0.09 us -> 13.4 us
  local copies, waits for them, and re-layouts: 8.78 us -> 0.15 us
    all_to_all x2 -> x0, blocking collectives: 111 us -> none  [the longest x1 57.7 us: body(): lax.all_to_all(outgoing, 'expert', split_axis=1, concat_axis=1, tiled=True)]
    reduce_scatter x0 -> x1, waiting for transfers between devices: none -> 83.4 us  [body(): lax.psum_scatter(weighted, 'expert', scatter_dimension=0, tiled=True)]
    all_gather x0 -> x1, waiting for transfers between devices: none -> 36 us  [body(): rows = lax.all_gather(hidden_in, 'expert', axis=0, tiled=True)]
    all_gather x0 -> x1, blocking collectives: none -> 24.1 us  [body(): weights = lax.all_gather(dense, 'expert', axis=0, tiled=True)]
    reshape x1 -> x0, local copies, waits for them, and re-layouts: 2.3 us -> none  [body(): outgoing = outgoing.astype(jnp.bfloat16).reshape(capacity, groups, width)]
    convert_element_type x1 -> x0, local copies, waits for them, and re-layouts: 2.3 us -> none  [body(): produced = jnp.einsum('cnf,fd->cnd', inner, w_out[0], preferred_element_t...]
    all_to_all x1 -> x0, local copies, waits for them, and re-layouts: 2.3 us -> none  [body(): lax.all_to_all(produced, 'expert', split_axis=1, concat_axis=1, tiled=True)]
    dot_general x5 -> x2, matrix products: 16.3 us -> 15 us  [the longest x1 10 us: body(): projected = jnp.dot(rows, w_in[0], preferred_element_type=jnp.float32)]
  transfers between devices with their start and end apart: 0 -> 2, of which waited for: 0 -> 2; matrix products, arithmetic and copies ran while one was open for 0% -> 1% of each run, Pallas kernels for 0% -> 0%
where the time goes in v1:
time: 174 us
  waiting for transfers between devices  120 us (69%)
  blocking collectives  24.1 us (14%)
  matrix products  15 us (9%)
  between operations  13.4 us (8%)
    reduce_scatter x1, waiting for transfers between devices, body(): lax.psum_scatter(weighted, 'expert', scatter_dimension=0, tiled=True)  83.4 us
    all_gather x1, waiting for transfers between devices, body(): rows = lax.all_gather(hidden_in, 'expert', axis=0, tiled=True)  36 us
    all_gather x1, blocking collectives, body(): weights = lax.all_gather(dense, 'expert', axis=0, tiled=True)  24.1 us
    dot_general x1, matrix products, body(): projected = jnp.dot(rows, w_in[0], preferred_element_type=jnp.float32)  10 us
    dot_general x1, matrix products, body(): jnp.dot(inner, w_out[0], preferred_element_type=jnp.float32)  5.04 us
  transfers between devices with their start and end apart: 2, of which 2 were waited for; matrix products, arithmetic and copies ran while one was open for 1% of the time, Pallas kernels for 0%

profile of v1, /device:TPU:64, one launch (start us, length us, event | category | flops | bytes accessed | tf_op | source)
XLA Modules:
  0.0 173.9 jit_solution(9898042919409677217)
XLA Ops:
  6.5 0.0 copy-start
  6.5 0.0 all-gather.3.cloned.1.call-start
  6.5 0.7 all-gather.3.cloned.1.call-update
  7.3 0.0 reduce-scatter.2.cloned.1.call-start
  7.3 0.9 select_reduce_fusion.1
  8.2 24.1 %all-gather = f32[16,64,16]{1,2,0:T(8,128)S(1)} all-gather(f32[1,64,16]{1,2,0:T(8,128)S(1)} %bitcast.10), channel_id=1, replica_groups=mesh['dp'=16,'expert'=16] {'expert'}, dimensions={0}, use_global_device_ids=true | all-gather | bytes 69632 | tf_op jit(solution)/shard_map/all_gather | solution.py:16
  32.3 0.1 reshape.9
  32.4 0.1 select_reduce_fusion
  32.5 36.0 %all-gather.3.cloned.1.call-done = bf16[1024,2048]{1,0:T(8,128)(2,1)} async-done(((bf16[64,2048]{1,0:T(8,128)(2,1)}), bf16[1024,2048]{1,0:T(8,128)(2,1)}) %all-gather.3.cloned.1.call-update) | async-done | bytes 4194320 | tf_op jit(solution)/shard_map/all_gather | solution.py:15
  68.6 10.0 %fusion = f32[1024,1536]{1,0:T(8,128)S(1)} fusion(bf16[1024,2048]{1,0:T(8,128)(2,1)} %all-gather.3.cloned.1.call-done, bf16[1,2048,1536]{2,1,0:T(8,128)(2,1)} %param.8), kind=kOutput, calls=%fused_computation.1 | convolution fusion | flops 6442450944 | bytes 16777216 | tf_op jit(solution)/shard_map/dot_general | solution.py:18
  78.6 0.0 copy-done
  78.6 5.0 %multiply_convert_fusion = bf16[1024,2048]{1,0:T(8,128)(2,1)} fusion(f32[1024]{0:T(1024)S(1)} %select_reduce_fusion, bf16[1,768,2048]{2,1,0:T(8,128)(2,1)S(1)} %copy-done, f32[1024,1536]{1,0:T(8,128)S(1)} %fusion), kind=kOutput, calls=%fused_computation | convolution fusion | flops 3234332672 | bytes 13635584 | tf_op jit(solution)/shard_map/dot_general | solution.py:20
  83.6 0.0 reduce-scatter.2.cloned.1.call-update
  83.7 83.4 %reduce-scatter.2.cloned.1.call-done = bf16[64,2048]{1,0:T(8,128)(2,1)} async-done(((bf16[1024,2048]{1,0:T(8,128)(2,1)}), bf16[64,2048]{1,0:T(8,128)(2,1)}) %reduce-scatter.2.cloned.1.call-update) | async-done | bytes 262160 | tf_op jit(solution)/shard_map/reduce_scatter | solution.py:22
  (2 shorter events, 0.0 us)
Async XLA Ops:
  6.5 72.0 %copy-start = (bf16[1,768,2048]{2,1,0:T(8,128)(2,1)S(1)}, bf16[1,768,2048]{2,1,0:T(8,128)(2,1)}, u32[]{:S(2)}) copy-start(bf16[1,768,2048]{2,1,0:T(8,128)(2,1)} %param.9) | copy-start | bytes 9437188
  6.5 62.0 %all-gather.3.cloned.1.call-start = ((), (), s32[]{:S(2)}) async-start(), calls=%async_computation.1 | async-start | bytes 4456448 | tf_op jit(solution)/shard_map/all_gather | solution.py:15
  7.3 159.8 %reduce-scatter.2.cloned.1.call-start = ((), (), s32[]{:S(2)}) async-start(), calls=%async_computation.2 | async-start | bytes 4456448 | tf_op jit(solution)/shard_map/reduce_scatter | solution.py:22
Sparse Core Ops, SparseCore 0:
  9.8 58.7 all-gather.2
  83.8 83.2 reduce-scatter.1

commit v2 on v1

v2 whole, which is shorter than its diff:
```python
import jax
import jax.numpy as jnp
import numpy as np
from jax import lax
from jax.sharding import Mesh
from jax.sharding import PartitionSpec as P

SIDE = 4
PAD = 128


def spread(block, axis):
    copies = jnp.broadcast_to(block[None], (SIDE,) + block.shape)
    return lax.all_to_all(copies, axis, 0, 0, tiled=False)


def collect(parts, axis):
    moved = lax.all_to_all(parts.astype(jnp.bfloat16), axis, 0, 0, tiled=False)
    return jnp.sum(moved.astype(jnp.float32), axis=0)


def body(hidden_in, route_ids, gates, w_in, w_out):
    me = lax.axis_index("ex") * SIDE + lax.axis_index("ey")
    count, width = hidden_in.shape
    half = w_out.shape[1]
    experts = jnp.arange(SIDE * SIDE, dtype=jnp.int32)
    table = jnp.sum(
        jnp.where(route_ids[:, :, None] == experts, gates[:, :, None], jnp.float32(0.0)), axis=1
    )
    high = table.astype(jnp.bfloat16)
    low = (table - high.astype(jnp.float32)).astype(jnp.bfloat16)
    extra = jnp.zeros((count, PAD - 2 * SIDE * SIDE), jnp.bfloat16)
    payload = jnp.concatenate([hidden_in, high, low, extra], axis=1)
    split = count // 2
    orders = (("ex", "ey"), ("ey", "ex"))
    gathered = []
    for i, (first, second) in enumerate(orders):
        own = payload[i * split:(i + 1) * split]
        stage = spread(own, first).reshape(SIDE * split, -1)
        gathered.append(spread(stage, second).reshape(SIDE * SIDE * split, -1))
    rows = jnp.concatenate(gathered, axis=0)
    picked = (experts == me)[None, :]
    got_high = rows[:, width:width + SIDE * SIDE].astype(jnp.float32)
    got_low = rows[:, width + SIDE * SIDE:width + 2 * SIDE * SIDE].astype(jnp.float32)
    mine = jnp.sum(jnp.where(picked, got_high + got_low, jnp.float32(0.0)), axis=1)
    projected = jnp.dot(rows[:, :width], w_in[0], preferred_element_type=jnp.float32)
    inner = (jax.nn.silu(projected[:, :half]) * projected[:, half:]).astype(jnp.bfloat16)
    produced = jnp.dot(inner, w_out[0], preferred_element_type=jnp.float32).astype(jnp.bfloat16)
    weighted = mine[:, None] * produced.astype(jnp.float32)
    outs = []
    for i, (first, second) in enumerate(orders):
        part = weighted[i * SIDE * SIDE * split:(i + 1) * SIDE * SIDE * split]
        stage = collect(part.reshape(SIDE, SIDE * split, width), second)
        outs.append(collect(stage.reshape(SIDE, split, width), first))
    return jnp.concatenate(outs, axis=0).astype(jnp.bfloat16)


def solution(mesh):
    grid = Mesh(mesh.devices.reshape(mesh.shape["dp"], SIDE, SIDE), ("dp", "ex", "ey"))
    rows = P(("dp", "ex", "ey"), None)
    placed = (rows, rows, rows, P(("ex", "ey"), None, None), P(("ex", "ey"), None, None))
    return jax.shard_map(body, mesh=grid, in_specs=placed, out_specs=rows, check_vma=False)
```

time: 174 us -> 198 us (1.14)
  waiting for transfers between devices: 120 us -> 76.5 us
  local copies, waits for them, and re-layouts: 0.15 us -> 31.4 us
  starting transfers between devices: 0.04 us -> 26 us
  blocking collectives: 24.1 us -> 39.5 us
  between operations: 13.4 us -> 0.13 us
  other arithmetic: 0.98 us -> 10.7 us
  matrix products: 15 us -> 12.9 us
    reduce_scatter x1 -> x0, waiting for transfers between devices: 83.4 us -> none  [body(): lax.psum_scatter(weighted, 'expert', scatter_dimension=0, tiled=True)]
    all_to_all x0 -> x6, waiting for transfers between devices: none -> 76.5 us  [the longest x3 45.9 us: spread(): return lax.all_to_all(copies, axis, 0, 0, tiled=False)]
    all_to_all x0 -> x2, blocking collectives: none -> 39.5 us  [the longest x1 25.3 us: collect(): moved = lax.all_to_all(parts.astype(jnp.bfloat16), axis, 0, 0, tiled=False)]
    all_gather x1 -> x0, waiting for transfers between devices: 36 us -> none  [body(): rows = lax.all_gather(hidden_in, 'expert', axis=0, tiled=True)]
    all_to_all x0 -> x6, starting transfers between devices: none -> 26 us  [the longest x3 13.2 us: spread(): return lax.all_to_all(copies, axis, 0, 0, tiled=False)]
    all_gather x1 -> x0, blocking collectives: 24.1 us -> none  [body(): weights = lax.all_gather(dense, 'expert', axis=0, tiled=True)]
    broadcast_in_dim x0 -> x7, local copies, waits for them, and re-layouts: none -> 10.5 us  [the longest x6 10.5 us: spread(): copies = jnp.broadcast_to(block[None], (SIDE,) + block.shape)]
    reduce_sum x1 -> x5, other arithmetic: 0.08 us -> 9.11 us  [the longest x4 8.11 us: collect(): return jnp.sum(moved.astype(jnp.float32), axis=0)]
  transfers between devices with their start and end apart: 2 -> 6, of which waited for: 2 -> 6; matrix products, arithmetic and copies ran while one was open for 1% -> 10% of each run, Pallas kernels for 0% -> 0%
where the time goes in v2:
time: 198 us; the launch traced here: 197 us
  waiting for transfers between devices  76.5 us (39%)
  blocking collectives  39.5 us (20%)
  local copies, waits for them, and re-layouts  31.4 us (16%)
  starting transfers between devices  26 us (13%)
  matrix products  12.9 us (7%)
  other arithmetic  10.7 us (5%)
    all_to_all x3, waiting for transfers between devices, spread(): return lax.all_to_all(copies, axis, 0, 0, tiled=False)  45.9 us
    all_to_all x3, waiting for transfers between devices, collect(): moved = lax.all_to_all(parts.astype(jnp.bfloat16), axis, 0, 0, tiled=False)  30.6 us
    all_to_all x1, blocking collectives, collect(): moved = lax.all_to_all(parts.astype(jnp.bfloat16), axis, 0, 0, tiled=False)  25.3 us
    all_to_all x1, blocking collectives, spread(): return lax.all_to_all(copies, axis, 0, 0, tiled=False)  14.2 us
    all_to_all x3, starting transfers between devices, spread(): return lax.all_to_all(copies, axis, 0, 0, tiled=False)  13.2 us
    all_to_all x3, starting transfers between devices, collect(): moved = lax.all_to_all(parts.astype(jnp.bfloat16), axis, 0, 0, tiled=False)  12.7 us
    broadcast_in_dim x6, local copies, waits for them, and re-layouts, spread(): copies = jnp.broadcast_to(block[None], (SIDE,) + block.shape)  10.5 us
    dot_general x1, matrix products, body(): jnp.dot(rows[:, :width], w_in[0], preferred_element_type=jnp.float32)  9.15 us
  transfers between devices with their start and end apart: 6, of which 6 were waited for; matrix products, arithmetic and copies ran while one was open for 10% of the time, Pallas kernels for 0%

profile of v2, /device:TPU:64, one launch (start us, length us, event | category | flops | bytes accessed | tf_op | source)
XLA Modules:
  0.0 197.2 jit_solution(615474951119493398)
XLA Ops:
  0.0 0.9 select_reduce_fusion.1
  1.1 1.0 concatenate.10
  2.2 14.2 %all_to_all.40 = bf16[4,32,2176]{2,1,0:T(8,128)(2,1)} all-to-all(bf16[4,32,2176]{2,1,0:T(8,128)(2,1)S(1)} %broadcast_in_dim.65), channel_id=1, replica_groups=mesh['dp'=16,'ex'=4,'ey'=4] {'ey'}, dimensions={0} | all-to-all | bytes 1114112 | tf_op jit(solution)/shard_map/all_to_all | solution.py:14
  17.3 4.3 %all-to-all-start = ((bf16[4,32,2176]{2,1,0:T(8,128)(2,1)}), bf16[4,32,2176]{2,1,0:T(8,128)(2,1)}, u32[]{:S(2)}, u32[]{:S(2)}) async-start(bf16[4,32,2176]{2,1,0:T(8,128)(2,1)} %broadcast_in_dim.62), calls=%async_computation | async-start | bytes 1114112 | tf_op jit(solution)/shard_map/all_to_all | solution.py:14
  21.6 2.1 %copy.33 = bf16[128,2176]{0,1:T(8,128)(2,1)} copy(bf16[128,2176]{1,0:T(8,128)(2,1)} %bitcast.18) | data formatting | bytes 1114112 | tf_op jit(solution)/shard_map/broadcast_in_dim | solution.py:13
  23.7 6.5 %all-to-all-done = bf16[4,32,2176]{2,1,0:T(8,128)(2,1)} async-done(((bf16[4,32,2176]{2,1,0:T(8,128)(2,1)}), bf16[4,32,2176]{2,1,0:T(8,128)(2,1)}, u32[]{:S(2)}, u32[]{:S(2)}) %all-to-all-start) | async-done | bytes 557088 | tf_op jit(solution)/shard_map/all_to_all | solution.py:14
  30.2 2.7 %broadcast_in_dim.67 = bf16[4,128,2176]{1,2,0:T(8,128)(2,1)} broadcast(bf16[128,2176]{0,1:T(8,128)(2,1)} %copy.33), dimensions={1,2} | broadcast | bytes 2785280 | tf_op jit(solution)/shard_map/broadcast_in_dim | solution.py:13
  32.9 4.5 %all-to-all-start.3 = ((bf16[4,128,2176]{1,2,0:T(8,128)(2,1)}), bf16[4,128,2176]{1,2,0:T(8,128)(2,1)}, u32[]{:S(2)}, u32[]{:S(2)}) async-start(bf16[4,128,2176]{1,2,0:T(8,128)(2,1)} %broadcast_in_dim.67), calls=%async_computation.3 | async-start | bytes 4456448 | tf_op jit(solution)/shard_map/all_to_all | solution.py:14
  37.4 2.1 %copy.31 = bf16[128,2176]{0,1:T(8,128)(2,1)} copy(bf16[128,2176]{1,0:T(8,128)(2,1)} %bitcast) | data formatting | bytes 1114112 | tf_op jit(solution)/shard_map/broadcast_in_dim | solution.py:13
  39.5 23.2 %all-to-all-done.3 = bf16[4,128,2176]{1,2,0:T(8,128)(2,1)} async-done(((bf16[4,128,2176]{1,2,0:T(8,128)(2,1)}), bf16[4,128,2176]{1,2,0:T(8,128)(2,1)}, u32[]{:S(2)}, u32[]{:S(2)}) %all-to-all-start.3) | async-done | bytes 2228256 | tf_op jit(solution)/shard_map/all_to_all | solution.py:14
  62.7 2.7 %broadcast_in_dim.64 = bf16[4,128,2176]{1,2,0:T(8,128)(2,1)} broadcast(bf16[128,2176]{0,1:T(8,128)(2,1)} %copy.31), dimensions={1,2} | broadcast | bytes 2785280 | tf_op jit(solution)/shard_map/broadcast_in_dim | solution.py:13
  65.4 4.5 %all-to-all-start.1 = ((bf16[4,128,2176]{1,2,0:T(8,128)(2,1)}), bf16[4,128,2176]{1,2,0:T(8,128)(2,1)}, u32[]{:S(2)}, u32[]{:S(2)}) async-start(bf16[4,128,2176]{1,2,0:T(8,128)(2,1)} %broadcast_in_dim.64), calls=%async_computation.1 | async-start | bytes 4456448 | tf_op jit(solution)/shard_map/all_to_all | solution.py:14
  69.9 4.2 %copy.34 = bf16[4,128,2176]{2,1,0:T(8,128)(2,1)} copy(bf16[4,128,2176]{1,2,0:T(8,128)(2,1)} %all-to-all-done.3) | data formatting | bytes 4456448 | tf_op jit(solution)/shard_map/all_to_all | solution.py:14
  74.1 4.1 %copy.36 = bf16[512,2176]{0,1:T(8,128)(2,1)} copy(bf16[512,2176]{1,0:T(8,128)(2,1)} %bitcast.14) | data formatting | bytes 4456448 | tf_op jit(solution)/shard_map/reshape | solution.py:40
  78.2 16.2 %all-to-all-done.1 = bf16[4,128,2176]{1,2,0:T(8,128)(2,1)} async-done(((bf16[4,128,2176]{1,2,0:T(8,128)(2,1)}), bf16[4,128,2176]{1,2,0:T(8,128)(2,1)}, u32[]{:S(2)}, u32[]{:S(2)}) %all-to-all-start.1) | async-done | bytes 2228256 | tf_op jit(solution)/shard_map/all_to_all | solution.py:14
  94.3 4.1 %copy.32 = bf16[4,128,2176]{2,1,0:T(8,128)(2,1)} copy(bf16[4,128,2176]{1,2,0:T(8,128)(2,1)} %all-to-all-done.1) | data formatting | bytes 4456448 | tf_op jit(solution)/shard_map/all_to_all | solution.py:14
  98.5 4.1 %copy.35 = bf16[512,2176]{0,1:T(8,128)(2,1)} copy(bf16[512,2176]{1,0:T(8,128)(2,1)} %bitcast.15) | data formatting | bytes 4456448 | tf_op jit(solution)/shard_map/reshape | solution.py:40
  102.6 1.0 select_reduce_fusion
  105.0 9.1 %fusion = f32[1024,1536]{1,0:T(8,128)S(1)} fusion(bf16[1,2048,1536]{2,1,0:T(8,128)(2,1)} %param.8, bf16[512,2176]{0,1:T(8,128)(2,1)S(1)} %copy-done.1, bf16[512,2176]{0,1:T(8,128)(2,1)S(1)} %copy-done.2), kind=kOutput, calls=%fused_computation.1 | convolution fusion | flops 6450839552 | bytes 17039360 | tf_op jit(solution)/shard_map/dot_general | solution.py:46
  114.1 3.8 %multiply_convert_fusion = bf16[1024,2048]{1,0:T(8,128)(2,1)S(1)} fusion(f32[1024]{0:T(1024)S(1)} %select_reduce_fusion, bf16[1,768,2048]{2,1,0:T(8,128)(2,1)S(1)} %copy-done, f32[1024,1536]{1,0:T(8,128)S(1)} %fusion), kind=kOutput, calls=%fused_computation | convolution fusion | flops 3234332672 | bytes 13635584 | tf_op jit(solution)/shard_map/dot_general | solution.py:48
  117.9 1.7 fusion.9
  119.6 25.3 %all_to_all.41 = bf16[4,128,2048]{2,1,0:T(8,128)(2,1)} all-to-all(bf16[4,128,2048]{2,1,0:T(8,128)(2,1)S(1)} %bitcast.17), channel_id=1, replica_groups=mesh['dp'=16,'ex'=4,'ey'=4] {'ex'}, dimensions={0} | all-to-all | bytes 4194304 | tf_op jit(solution)/shard_map/all_to_all | solution.py:18
  145.0 4.4 %all-to-all-start.4 = ((bf16[4,128,2048]{2,1,0:T(8,128)(2,1)}), bf16[4,128,2048]{2,1,0:T(8,128)(2,1)}, u32[]{:S(2)}, u32[]{:S(2)}) async-start(bf16[4,128,2048]{2,1,0:T(8,128)(2,1)} %bitcast.16), calls=%async_computation.4 | async-start | bytes 4194304 | tf_op jit(solution)/shard_map/all_to_all | solution.py:18
  149.4 2.9 %reduce_sum.64 = bf16[128,2048]{1,0:T(8,128)(2,1)} reduce(bf16[4,128,2048]{2,1,0:T(8,128)(2,1)} %all_to_all.41, bf16[]{:T(256)} %constant.16.clone.1), dimensions={0}, to_apply=%region_4.5 | reduce | flops 786432 | bytes 2621442 | tf_op jit(solution)/shard_map/reduce_sum | solution.py:19
  152.4 18.4 %all-to-all-done.4 = bf16[4,128,2048]{2,1,0:T(8,128)(2,1)} async-done(((bf16[4,128,2048]{2,1,0:T(8,128)(2,1)}), bf16[4,128,2048]{2,1,0:T(8,128)(2,1)}, u32[]{:S(2)}, u32[]{:S(2)}) %all-to-all-start.4) | async-done | bytes 2097184 | tf_op jit(solution)/shard_map/all_to_all | solution.py:18
  170.8 4.2 %all-to-all-start.7 = ((bf16[4,32,2048]{2,1,0:T(8,128)(2,1)}), bf16[4,32,2048]{2,1,0:T(8,128)(2,1)}, u32[]{:S(2)}, u32[]{:S(2)}) async-start(bf16[4,32,2048]{2,1,0:T(8,128)(2,1)} %bitcast.19), calls=%async_computation.7 | async-start | bytes 1048576 | tf_op jit(solution)/shard_map/all_to_all | solution.py:18
  174.9 2.9 %reduce_sum.62 = bf16[128,2048]{1,0:T(8,128)(2,1)} reduce(bf16[4,128,2048]{2,1,0:T(8,128)(2,1)} %all-to-all-done.4, bf16[]{:T(256)} %constant.16.clone.1), dimensions={0}, to_apply=%region_2.3 | reduce | flops 786432 | bytes 2621442 | tf_op jit(solution)/shard_map/reduce_sum | solution.py:19
  177.9 5.2 %all-to-all-done.7 = bf16[4,32,2048]{2,1,0:T(8,128)(2,1)} async-done(((bf16[4,32,2048]{2,1,0:T(8,128)(2,1)}), bf16[4,32,2048]{2,1,0:T(8,128)(2,1)}, u32[]{:S(2)}, u32[]{:S(2)}) %all-to-all-start.7) | async-done | bytes 524320 | tf_op jit(solution)/shard_map/all_to_all | solution.py:18
  183.1 4.1 %all-to-all-start.5 = ((bf16[4,32,2048]{2,1,0:T(8,128)(2,1)}), bf16[4,32,2048]{2,1,0:T(8,128)(2,1)}, u32[]{:S(2)}, u32[]{:S(2)}) async-start(bf16[4,32,2048]{2,1,0:T(8,128)(2,1)} %bitcast.20), calls=%async_computation.5 | async-start | bytes 1048576 | tf_op jit(solution)/shard_map/all_to_all | solution.py:18
  187.2 1.1 reduce.3
  188.3 7.0 %all-to-all-done.5 = bf16[4,32,2048]{2,1,0:T(8,128)(2,1)} async-done(((bf16[4,32,2048]{2,1,0:T(8,128)(2,1)}), bf16[4,32,2048]{2,1,0:T(8,128)(2,1)}, u32[]{:S(2)}, u32[]{:S(2)}) %all-to-all-start.5) | async-done | bytes 524320 | tf_op jit(solution)/shard_map/all_to_all | solution.py:18
  195.4 1.1 reduce.2
  (15 shorter events, 3.2 us)
Async XLA Ops:
  0.0 114.1 %copy-start = (bf16[1,768,2048]{2,1,0:T(8,128)(2,1)S(1)}, bf16[1,768,2048]{2,1,0:T(8,128)(2,1)}, u32[]{:S(2)}) copy-start(bf16[1,768,2048]{2,1,0:T(8,128)(2,1)} %param.9) | copy-start | bytes 9437188
  17.3 12.9 %all-to-all-start = ((bf16[4,32,2176]{2,1,0:T(8,128)(2,1)}), bf16[4,32,2176]{2,1,0:T(8,128)(2,1)}, u32[]{:S(2)}, u32[]{:S(2)}) async-start(bf16[4,32,2176]{2,1,0:T(8,128)(2,1)} %broadcast_in_dim.62), calls=%async_computation | async-start | bytes 1114112 | tf_op jit(solution)/shard_map/all_to_all | solution.py:14
  32.9 29.8 %all-to-all-start.3 = ((bf16[4,128,2176]{1,2,0:T(8,128)(2,1)}), bf16[4,128,2176]{1,2,0:T(8,128)(2,1)}, u32[]{:S(2)}, u32[]{:S(2)}) async-start(bf16[4,128,2176]{1,2,0:T(8,128)(2,1)} %broadcast_in_dim.67), calls=%async_computation.3 | async-start | bytes 4456448 | tf_op jit(solution)/shard_map/all_to_all | solution.py:14
  65.4 28.9 %all-to-all-start.1 = ((bf16[4,128,2176]{1,2,0:T(8,128)(2,1)}), bf16[4,128,2176]{1,2,0:T(8,128)(2,1)}, u32[]{:S(2)}, u32[]{:S(2)}) async-start(bf16[4,128,2176]{1,2,0:T(8,128)(2,1)} %broadcast_in_dim.64), calls=%async_computation.1 | async-start | bytes 4456448 | tf_op jit(solution)/shard_map/all_to_all | solution.py:14
  102.6 1.7 copy-start.1
  102.6 2.4 %copy-start.2 = (bf16[512,2176]{0,1:T(8,128)(2,1)S(1)}, bf16[512,2176]{0,1:T(8,128)(2,1)}, u32[]{:S(2)}) copy-start(bf16[512,2176]{0,1:T(8,128)(2,1)} %copy.35) | copy-start | bytes 6684676
  145.0 25.8 %all-to-all-start.4 = ((bf16[4,128,2048]{2,1,0:T(8,128)(2,1)}), bf16[4,128,2048]{2,1,0:T(8,128)(2,1)}, u32[]{:S(2)}, u32[]{:S(2)}) async-start(bf16[4,128,2048]{2,1,0:T(8,128)(2,1)} %bitcast.16), calls=%async_computation.4 | async-start | bytes 4194304 | tf_op jit(solution)/shard_map/all_to_all | solution.py:18
  170.8 12.3 %all-to-all-start.7 = ((bf16[4,32,2048]{2,1,0:T(8,128)(2,1)}), bf16[4,32,2048]{2,1,0:T(8,128)(2,1)}, u32[]{:S(2)}, u32[]{:S(2)}) async-start(bf16[4,32,2048]{2,1,0:T(8,128)(2,1)} %bitcast.19), calls=%async_computation.7 | async-start | bytes 1048576 | tf_op jit(solution)/shard_map/all_to_all | solution.py:18
  183.1 12.3 %all-to-all-start.5 = ((bf16[4,32,2048]{2,1,0:T(8,128)(2,1)}), bf16[4,32,2048]{2,1,0:T(8,128)(2,1)}, u32[]{:S(2)}, u32[]{:S(2)}) async-start(bf16[4,32,2048]{2,1,0:T(8,128)(2,1)} %bitcast.20), calls=%async_computation.5 | async-start | bytes 1048576 | tf_op jit(solution)/shard_map/all_to_all | solution.py:18

commit v3 on v1

v3 whole, which is shorter than its diff:
```python
import jax
import jax.numpy as jnp
from jax import lax
from jax.sharding import PartitionSpec as P

CHUNKS = 2


def slot_ranks(choices, count):
    flat = choices.reshape(-1)
    length = flat.shape[0]
    onehot = (flat[:, None] == jnp.arange(count, dtype=jnp.int32)).astype(jnp.bfloat16)
    lower = (
        jnp.arange(length, dtype=jnp.int32)[:, None] > jnp.arange(length, dtype=jnp.int32)[None, :]
    ).astype(jnp.bfloat16)
    ranks = jnp.dot(lower, onehot, preferred_element_type=jnp.float32)
    picked = jnp.sum(ranks * onehot.astype(jnp.float32), axis=-1)
    return picked.astype(jnp.int32).reshape(choices.shape)


def body(hidden_in, route_ids, gates, w_in, w_out):
    groups = lax.axis_size("expert")
    rows_here, width = hidden_in.shape
    half = w_out.shape[1]
    capacity = rows_here
    per_chunk = capacity // CHUNKS
    slots_all = capacity * groups
    rank = slot_ranks(route_ids, groups)
    chunk = rank // per_chunk
    slot = chunk * (groups * per_chunk) + route_ids * per_chunk + rank % per_chunk
    hit = slot[:, :, None] == jnp.arange(slots_all, dtype=jnp.int32)
    placement = jnp.sum(hit.astype(jnp.bfloat16), axis=1)
    weighting = jnp.sum(jnp.where(hit, gates[:, :, None], jnp.float32(0.0)), axis=1)
    high = weighting.astype(jnp.bfloat16)
    low = (weighting - high.astype(jnp.float32)).astype(jnp.bfloat16)
    outgoing = jnp.dot(placement.T, hidden_in, preferred_element_type=jnp.float32)
    outgoing = outgoing.astype(jnp.bfloat16).reshape(CHUNKS, groups, per_chunk, width)
    total = jnp.zeros((rows_here, width), jnp.float32)
    for c in range(CHUNKS):
        arrived = lax.all_to_all(outgoing[c], "expert", 0, 0, tiled=False)
        projected = jnp.dot(
            arrived.reshape(groups * per_chunk, width), w_in[0], preferred_element_type=jnp.float32
        )
        inner = (jax.nn.silu(projected[:, :half]) * projected[:, half:]).astype(jnp.bfloat16)
        produced = jnp.dot(inner, w_out[0], preferred_element_type=jnp.float32).astype(jnp.bfloat16)
        returned = lax.all_to_all(
            produced.reshape(groups, per_chunk, width), "expert", 0, 0, tiled=False
        ).reshape(groups * per_chunk, width)
        cols = slice(c * groups * per_chunk, (c + 1) * groups * per_chunk)
        total = total + jnp.dot(high[:, cols], returned, preferred_element_type=jnp.float32)
        total = total + jnp.dot(low[:, cols], returned, preferred_element_type=jnp.float32)
    return total.astype(jnp.bfloat16)


def solution(mesh):
    placed = (
        P(("dp", "expert"), None),
        P(("dp", "expert"), None),
        P(("dp", "expert"), None),
        P("expert", None, None),
        P("expert", None, None),
    )
    return jax.shard_map(
        body, mesh=mesh, in_specs=placed, out_specs=P(("dp", "expert"), None), check_vma=False
    )
```

time: 174 us -> 142 us (0.82)
  waiting for transfers between devices: 120 us -> 56.3 us
  matrix products: 15 us -> 31.1 us
  starting transfers between devices: 0.04 us -> 13.9 us
  between operations: 13.4 us -> 0.12 us
  blocking collectives: 24.1 us -> 35.2 us
  local copies, waits for them, and re-layouts: 0.15 us -> 3.22 us
    reduce_scatter x1 -> x0, waiting for transfers between devices: 83.4 us -> none  [body(): lax.psum_scatter(weighted, 'expert', scatter_dimension=0, tiled=True)]
    all_to_all x0 -> x3, waiting for transfers between devices: none -> 56.3 us  [the longest x2 37 us: body(): lax.all_to_all(produced.reshape(groups, per_chunk, width), 'expert', 0, 0...]
    all_gather x1 -> x0, waiting for transfers between devices: 36 us -> none  [body(): rows = lax.all_gather(hidden_in, 'expert', axis=0, tiled=True)]
    all_to_all x0 -> x1, blocking collectives: none -> 35.2 us  [body(): arrived = lax.all_to_all(outgoing[c], 'expert', 0, 0, tiled=False)]
    all_gather x1 -> x0, blocking collectives: 24.1 us -> none  [body(): weights = lax.all_gather(dense, 'expert', axis=0, tiled=True)]
    dot_general x1 -> x8, matrix products: 10 us -> 24.7 us  [the longest x2 12.3 us: body(): jnp.dot(arrived.reshape(groups * per_chunk, width), w_in[0], preferred_el...]
    all_to_all x0 -> x3, starting transfers between devices: none -> 13.9 us  [the longest x2 9.41 us: body(): lax.all_to_all(produced.reshape(groups, per_chunk, width), 'expert', 0, 0...]
    slice x0 -> x1, local copies, waits for them, and re-layouts: none -> 1.89 us  [body(): arrived = lax.all_to_all(outgoing[c], 'expert', 0, 0, tiled=False)]
  transfers between devices with their start and end apart: 2 -> 3, of which waited for: 2 -> 3; matrix products, arithmetic and copies ran while one was open for 1% -> 17% of each run, Pallas kernels for 0% -> 0%
where the time goes in v3:
time: 142 us
  waiting for transfers between devices  56.3 us (40%)
  blocking collectives  35.2 us (25%)
  matrix products  31.1 us (22%)
  starting transfers between devices  13.9 us (10%)
  local copies, waits for them, and re-layouts  3.22 us (2%)
  other arithmetic  2.14 us (2%)
    all_to_all x2, waiting for transfers between devices, body(): lax.all_to_all(produced.reshape(groups, per_chunk, width), 'expert', 0, 0...  37 us
    all_to_all x1, blocking collectives, body(): arrived = lax.all_to_all(outgoing[c], 'expert', 0, 0, tiled=False)  35.2 us
    all_to_all x1, waiting for transfers between devices, body(): arrived = lax.all_to_all(outgoing[c], 'expert', 0, 0, tiled=False)  19.3 us
    dot_general x2, matrix products, body(): jnp.dot(arrived.reshape(groups * per_chunk, width), w_in[0], preferred_el...  12.3 us
    all_to_all x2, starting transfers between devices, body(): lax.all_to_all(produced.reshape(groups, per_chunk, width), 'expert', 0, 0...  9.41 us
    dot_general x2, matrix products, body(): jnp.dot(inner, w_out[0], preferred_element_type=jnp.float32)  6.36 us
    dot_general x2, matrix products, body(): jnp.dot(low[:, cols], returned, preferred_element_type=jnp.float32)  5.65 us
    all_to_all x1, starting transfers between devices, body(): arrived = lax.all_to_all(outgoing[c], 'expert', 0, 0, tiled=False)  4.45 us
  transfers between devices with their start and end apart: 3, of which 3 were waited for; matrix products, arithmetic and copies ran while one was open for 17% of the time, Pallas kernels for 0%

profile of v3, /device:TPU:64, one launch (start us, length us, event | category | flops | bytes accessed | tf_op | source)
XLA Modules:
  0.0 141.9 jit_solution(9416539267066420454)
XLA Ops:
  0.0 0.0 copy-start
  0.0 0.9 copy.16
  0.9 0.1 eq.30
  1.0 0.3 fusion.18
  1.3 0.1 convert_element_type.49
  1.4 0.1 copy.17
  1.5 0.7 fusion.33
  2.2 0.1 copy.21
  2.3 0.7 fusion.19
  2.9 2.2 %convolution_convert_fusion = bf16[1024,2048]{1,0:T(8,128)(2,1)S(1)} fusion(bf16[64,1024]{1,0:T(8,128)(2,1)S(1)} %fusion.19, bf16[64,2048]{1,0:T(8,128)(2,1)} %param.5), kind=kOutput, calls=%fused_computation.4 | convolution fusion | flops 270532608 | bytes 4587520 | tf_op jit(solution)/shard_map/dot_general | solution.py:36
  5.2 1.9 %fusion.40 = (bf16[512,2048]{1,0:T(8,128)(2,1)}, bf16[512,2048]{1,0:T(8,128)(2,1)S(1)}) fusion(bf16[1024,2048]{1,0:T(8,128)(2,1)S(1)} %convolution_convert_fusion), kind=kLoop, calls=%fused_computation.52 | loop fusion | bytes 8388608 | tf_op jit(solution)/shard_map/slice | solution.py:40
  7.1 35.2 %all_to_all.20 = bf16[16,32,2048]{2,1,0:T(8,128)(2,1)} all-to-all(bf16[16,32,2048]{2,1,0:T(8,128)(2,1)S(1)} %bitcast.31), channel_id=1, replica_groups=mesh['dp'=16,'expert'=16] {'expert'}, dimensions={0} | all-to-all | bytes 4194304 | tf_op jit(solution)/shard_map/all_to_all | solution.py:40
  42.2 4.4 %all-to-all-start.2 = ((bf16[16,32,2048]{2,1,0:T(8,128)(2,1)}), bf16[16,32,2048]{2,1,0:T(8,128)(2,1)}, u32[]{:S(2)}, u32[]{:S(2)}) async-start(bf16[16,32,2048]{2,1,0:T(8,128)(2,1)} %bitcast.30), calls=%async_computation.2 | async-start | bytes 4194304 | tf_op jit(solution)/shard_map/all_to_all | solution.py:40
  46.7 6.2 %fusion.2 = f32[512,1536]{1,0:T(8,128)S(1)} fusion(bf16[512,2048]{1,0:T(8,128)(2,1)} %bitcast.34, bf16[1,2048,1536]{2,1,0:T(8,128)(2,1)} %param.8), kind=kOutput, calls=%fused_computation.2 | convolution fusion | flops 3221225472 | bytes 11534336 | tf_op jit(solution)/shard_map/dot_general | solution.py:41
  52.9 0.0 copy-done
  52.9 3.2 %fusion.8 = bf16[512,2048]{1,0:T(8,128)(2,1)} fusion(bf16[1,768,2048]{2,1,0:T(8,128)(2,1)S(1)} %copy-done, f32[512,1536]{1,0:T(8,128)S(1)} %fusion.2), kind=kOutput, calls=%fused_computation.9 | convolution fusion | flops 1614020608 | bytes 8388608 | tf_op jit(solution)/shard_map/dot_general | solution.py:45
  56.1 19.3 %all-to-all-done.2 = bf16[16,32,2048]{2,1,0:T(8,128)(2,1)} async-done(((bf16[16,32,2048]{2,1,0:T(8,128)(2,1)}), bf16[16,32,2048]{2,1,0:T(8,128)(2,1)}, u32[]{:S(2)}, u32[]{:S(2)}) %all-to-all-start.2) | async-done | bytes 2097184 | tf_op jit(solution)/shard_map/all_to_all | solution.py:40
  75.4 4.4 %all-to-all-start.1 = ((bf16[16,32,2048]{2,1,0:T(8,128)(2,1)}), bf16[16,32,2048]{2,1,0:T(8,128)(2,1)}, u32[]{:S(2)}, u32[]{:S(2)}) async-start(bf16[16,32,2048]{2,1,0:T(8,128)(2,1)} %bitcast.33), calls=%async_computation.1 | async-start | bytes 4194304 | tf_op jit(solution)/shard_map/all_to_all | solution.py:46
  79.8 6.2 %fusion = f32[512,1536]{1,0:T(8,128)S(1)} fusion(bf16[512,2048]{1,0:T(8,128)(2,1)} %bitcast.7, bf16[1,2048,1536]{2,1,0:T(8,128)(2,1)} %param.8), kind=kOutput, calls=%fused_computation | convolution fusion | flops 3221225472 | bytes 11534336 | tf_op jit(solution)/shard_map/dot_general | solution.py:41
  86.0 3.2 %fusion.11 = bf16[512,2048]{1,0:T(8,128)(2,1)} fusion(bf16[1,768,2048]{2,1,0:T(8,128)(2,1)S(1)} %copy-done, f32[512,1536]{1,0:T(8,128)S(1)} %fusion), kind=kOutput, calls=%fused_computation.10 | convolution fusion | flops 1614020608 | bytes 8388608 | tf_op jit(solution)/shard_map/dot_general | solution.py:45
  89.2 17.6 %all-to-all-done.1 = bf16[16,32,2048]{2,1,0:T(8,128)(2,1)} async-done(((bf16[16,32,2048]{2,1,0:T(8,128)(2,1)}), bf16[16,32,2048]{2,1,0:T(8,128)(2,1)}, u32[]{:S(2)}, u32[]{:S(2)}) %all-to-all-start.1) | async-done | bytes 2097184 | tf_op jit(solution)/shard_map/all_to_all | solution.py:46
  106.8 0.0 copy-start.1
  106.8 5.0 %all-to-all-start.3 = ((bf16[16,32,2048]{2,1,0:T(8,128)(2,1)}), bf16[16,32,2048]{2,1,0:T(8,128)(2,1)}, u32[]{:S(2)}, u32[]{:S(2)}) async-start(bf16[16,32,2048]{2,1,0:T(8,128)(2,1)} %bitcast.32), calls=%async_computation.3 | async-start | bytes 4194304 | tf_op jit(solution)/shard_map/all_to_all | solution.py:46
  111.8 0.0 copy-done.1
  111.8 0.1 copy.22
  111.9 0.7 select_reduce_fusion
  112.7 2.1 %fusion.27 = f32[64,2048]{1,0:T(8,128)S(1)} fusion(bf16[512,2048]{1,0:T(8,128)(2,1)} %bitcast.5, bf16[64,1024]{1,0:T(8,128)(2,1)S(1)} %get-tuple-element.6), kind=kOutput, calls=%fused_computation.32 | convolution fusion | flops 134217728 | bytes 2686976 | tf_op jit(solution)/shard_map/dot_general | solution.py:50
  114.7 2.9 %convolution_add_fusion.2 = f32[64,2048]{1,0:T(8,128)} fusion(f32[64,2048]{1,0:T(8,128)S(1)} %fusion.27, bf16[512,2048]{1,0:T(8,128)(2,1)} %bitcast.5, bf16[64,1024]{1,0:T(8,128)(2,1)S(1)} %get-tuple-element.5), kind=kOutput, calls=%fused_computation.13 | convolution fusion | flops 134348800 | bytes 3211264 | tf_op jit(solution)/shard_map/dot_general | solution.py:51
  117.6 19.4 %all-to-all-done.3 = bf16[16,32,2048]{2,1,0:T(8,128)(2,1)} async-done(((bf16[16,32,2048]{2,1,0:T(8,128)(2,1)}), bf16[16,32,2048]{2,1,0:T(8,128)(2,1)}, u32[]{:S(2)}, u32[]{:S(2)}) %all-to-all-start.3) | async-done | bytes 2097184 | tf_op jit(solution)/shard_map/all_to_all | solution.py:46
  137.0 2.2 %convolution_add_fusion.1 = f32[64,2048]{1,0:T(8,128)S(1)} fusion(f32[64,2048]{1,0:T(8,128)} %convolution_add_fusion.2, bf16[512,2048]{1,0:T(8,128)(2,1)} %bitcast.9, bf16[64,1024]{1,0:T(8,128)(2,1)S(1)} %get-tuple-element.6), kind=kOutput, calls=%fused_computation.12 | convolution fusion | flops 134348800 | bytes 3211264 | tf_op jit(solution)/shard_map/dot_general | solution.py:50
  139.1 2.8 %fusion.14 = bf16[64,2048]{1,0:T(8,128)(2,1)} fusion(f32[64,2048]{1,0:T(8,128)S(1)} %convolution_add_fusion.1, bf16[512,2048]{1,0:T(8,128)(2,1)} %bitcast.9, bf16[64,1024]{1,0:T(8,128)(2,1)S(1)} %get-tuple-element.5), kind=kOutput, calls=%fused_computation.14 | convolution fusion | flops 134479872 | bytes 2949120 | tf_op jit(solution)/shard_map/dot_general | solution.py:51
  (2 shorter events, 0.0 us)
Async XLA Ops:
  0.0 52.9 %copy-start = (bf16[1,768,2048]{2,1,0:T(8,128)(2,1)S(1)}, bf16[1,768,2048]{2,1,0:T(8,128)(2,1)}, u32[]{:S(2)}) copy-start(bf16[1,768,2048]{2,1,0:T(8,128)(2,1)} %param.9) | copy-start | bytes 9437188
  42.2 33.1 %all-to-all-start.2 = ((bf16[16,32,2048]{2,1,0:T(8,128)(2,1)}), bf16[16,32,2048]{2,1,0:T(8,128)(2,1)}, u32[]{:S(2)}, u32[]{:S(2)}) async-start(bf16[16,32,2048]{2,1,0:T(8,128)(2,1)} %bitcast.30), calls=%async_computation.2 | async-start | bytes 4194304 | tf_op jit(solution)/shard_map/all_to_all | solution.py:40
  75.4 31.4 %all-to-all-start.1 = ((bf16[16,32,2048]{2,1,0:T(8,128)(2,1)}), bf16[16,32,2048]{2,1,0:T(8,128)(2,1)}, u32[]{:S(2)}, u32[]{:S(2)}) async-start(bf16[16,32,2048]{2,1,0:T(8,128)(2,1)} %bitcast.33), calls=%async_computation.1 | async-start | bytes 4194304 | tf_op jit(solution)/shard_map/all_to_all | solution.py:46
  106.8 5.0 %copy-start.1 = (f32[64,8]{0,1:T(8,128)S(1)}, f32[64,8]{0,1:T(8,128)}, u32[]{:S(2)}) copy-start(f32[64,8]{0,1:T(8,128)} %param.7) | copy-start | bytes 6148
  106.8 30.1 %all-to-all-start.3 = ((bf16[16,32,2048]{2,1,0:T(8,128)(2,1)}), bf16[16,32,2048]{2,1,0:T(8,128)(2,1)}, u32[]{:S(2)}, u32[]{:S(2)}) async-start(bf16[16,32,2048]{2,1,0:T(8,128)(2,1)} %bitcast.32), calls=%async_computation.3 | async-start | bytes 4194304 | tf_op jit(solution)/shard_map/all_to_all | solution.py:46

commit v4 on v3

--- a/solution.py
+++ b/solution.py
@@ -3,7 +3,7 @@
 from jax import lax
 from jax.sharding import PartitionSpec as P
 
-CHUNKS = 2
+CHUNKS = 1
 
 
 def slot_ranks(choices, count):
@@ -31,8 +31,6 @@
     hit = slot[:, :, None] == jnp.arange(slots_all, dtype=jnp.int32)
     placement = jnp.sum(hit.astype(jnp.bfloat16), axis=1)
     weighting = jnp.sum(jnp.where(hit, gates[:, :, None], jnp.float32(0.0)), axis=1)
-    high = weighting.astype(jnp.bfloat16)
-    low = (weighting - high.astype(jnp.float32)).astype(jnp.bfloat16)
     outgoing = jnp.dot(placement.T, hidden_in, preferred_element_type=jnp.float32)
     outgoing = outgoing.astype(jnp.bfloat16).reshape(CHUNKS, groups, per_chunk, width)
     total = jnp.zeros((rows_here, width), jnp.float32)
@@ -47,8 +45,9 @@
             produced.reshape(groups, per_chunk, width), "expert", 0, 0, tiled=False
         ).reshape(groups * per_chunk, width)
         cols = slice(c * groups * per_chunk, (c + 1) * groups * per_chunk)
-        total = total + jnp.dot(high[:, cols], returned, preferred_element_type=jnp.float32)
-        total = total + jnp.dot(low[:, cols], returned, preferred_element_type=jnp.float32)
+        total = total + jnp.dot(
+            weighting[:, cols], returned.astype(jnp.float32), precision=lax.Precision.HIGHEST
+        )
     return total.astype(jnp.bfloat16)
 
 

time: 142 us -> 139 us (0.979)
  blocking collectives: 35.2 us -> 57.7 us
  matrix products: 31.1 us -> 19.6 us
  starting transfers between devices: 13.9 us -> 4.66 us
  waiting for transfers between devices: 56.3 us -> 53.5 us
  local copies, waits for them, and re-layouts: 3.22 us -> 1.35 us
    all_to_all x1, blocking collectives: 35.2 us -> 57.7 us  [body(): arrived = lax.all_to_all(outgoing[c], 'expert', 0, 0, tiled=False)]
    all_to_all x1 -> x0, waiting for transfers between devices: 19.3 us -> none  [body(): arrived = lax.all_to_all(outgoing[c], 'expert', 0, 0, tiled=False)]
    all_to_all x2 -> x1, waiting for transfers between devices: 37 us -> 53.5 us  [body(): lax.all_to_all(produced.reshape(groups, per_chunk, width), 'expert', 0, 0...]
    dot_general x2 -> x1, matrix products: 12.3 us -> 6.64 us  [body(): jnp.dot(arrived.reshape(groups * per_chunk, width), w_in[0], preferred_el...]
    all_to_all x2 -> x1, starting transfers between devices: 9.41 us -> 4.66 us  [body(): lax.all_to_all(produced.reshape(groups, per_chunk, width), 'expert', 0, 0...]
    dot_general x4 -> x1, matrix products: 9.87 us -> 5.19 us  [body(): jnp.dot(weighting[:, cols], returned.astype(jnp.float32), precision=lax.P...]
    all_to_all x1 -> x0, starting transfers between devices: 4.45 us -> none  [body(): arrived = lax.all_to_all(outgoing[c], 'expert', 0, 0, tiled=False)]
    slice x1 -> x0, local copies, waits for them, and re-layouts: 1.89 us -> none  [body(): arrived = lax.all_to_all(outgoing[c], 'expert', 0, 0, tiled=False)]
  transfers between devices with their start and end apart: 3 -> 1, of which waited for: 3 -> 1; matrix products, arithmetic and copies ran while one was open for 17% -> 1% of each run, Pallas kernels for 0% -> 0%
where the time goes in v4:
time: 139 us
  blocking collectives  57.7 us (42%)
  waiting for transfers between devices  53.5 us (38%)
  matrix products  19.6 us (14%)
  starting transfers between devices  4.66 us (3%)
  other arithmetic  2.11 us (2%)
    all_to_all x1, blocking collectives, body(): arrived = lax.all_to_all(outgoing[c], 'expert', 0, 0, tiled=False)  57.7 us
    all_to_all x1, waiting for transfers between devices, body(): lax.all_to_all(produced.reshape(groups, per_chunk, width), 'expert', 0, 0...  53.5 us
    dot_general x1, matrix products, body(): jnp.dot(arrived.reshape(groups * per_chunk, width), w_in[0], preferred_el...  6.64 us
    dot_general x1, matrix products, body(): jnp.dot(weighting[:, cols], returned.astype(jnp.float32), precision=lax.P...  5.19 us
    dot_general x1, matrix products, body(): jnp.dot(inner, w_out[0], preferred_element_type=jnp.float32)  5.08 us
    all_to_all x1, starting transfers between devices, body(): lax.all_to_all(produced.reshape(groups, per_chunk, width), 'expert', 0, 0...  4.66 us
  transfers between devices with their start and end apart: 1, of which 1 were waited for; matrix products, arithmetic and copies ran while one was open for 1% of the time, Pallas kernels for 0%

profile of v4, /device:TPU:64, one launch (start us, length us, event | category | flops | bytes accessed | tf_op | source)
XLA Modules:
  0.0 139.0 jit_solution(4423210897945629751)
XLA Ops:
  0.0 0.0 copy-start
  0.0 0.9 copy.16
  0.9 0.1 eq.30
  1.0 0.3 fusion.7
  1.3 0.1 convert_element_type.35
  1.4 0.1 copy.17
  1.5 0.7 fusion.13
  2.2 0.1 copy.21
  2.3 0.7 fusion.8
  2.9 0.0 slice-start
  3.0 2.4 %convolution_convert_fusion.1 = bf16[1024,2048]{1,0:T(8,128)(2,1)S(1)} fusion(bf16[64,1024]{1,0:T(8,128)(2,1)S(1)} %fusion.8, bf16[64,2048]{1,0:T(8,128)(2,1)} %param.5), kind=kOutput, calls=%fused_computation.3 | convolution fusion | flops 270532608 | bytes 4587520 | tf_op jit(solution)/shard_map/dot_general | solution.py:34
  5.3 0.0 slice-start.1
  5.4 57.7 %all_to_all.10 = bf16[16,64,2048]{2,1,0:T(8,128)(2,1)S(1)} all-to-all(bf16[16,64,2048]{2,1,0:T(8,128)(2,1)S(1)} %bitcast.15), channel_id=1, replica_groups=mesh['dp'=16,'expert'=16] {'expert'}, dimensions={0} | all-to-all | bytes 8388608 | tf_op jit(solution)/shard_map/all_to_all | solution.py:38
  63.0 0.0 slice-done
  63.0 0.0 slice-done.1
  63.1 6.6 %fusion = f32[1024,1536]{1,0:T(8,128)S(1)} fusion(bf16[1024,2048]{1,0:T(8,128)(2,1)S(1)} %bitcast.17, bf16[1,2048,1536]{2,1,0:T(8,128)(2,1)S(1)} %bitcast.19), kind=kOutput, calls=%fused_computation | convolution fusion | flops 6442450944 | bytes 16777216 | tf_op jit(solution)/shard_map/dot_general | solution.py:39
  69.7 0.0 copy-done
  69.7 5.1 %convolution_convert_fusion = bf16[1024,2048]{1,0:T(8,128)(2,1)} fusion(bf16[1,768,2048]{2,1,0:T(8,128)(2,1)S(1)} %copy-done, f32[1024,1536]{1,0:T(8,128)S(1)} %fusion), kind=kOutput, calls=%fused_computation.2 | convolution fusion | flops 3228041216 | bytes 13631488 | tf_op jit(solution)/shard_map/dot_general | solution.py:43
  74.8 0.0 copy-start.1
  74.8 4.7 %all-to-all-start.1 = ((bf16[16,64,2048]{2,1,0:T(8,128)(2,1)}), bf16[16,64,2048]{2,1,0:T(8,128)(2,1)}, u32[]{:S(2)}, u32[]{:S(2)}) async-start(bf16[16,64,2048]{2,1,0:T(8,128)(2,1)} %bitcast.16), calls=%async_computation.1 | async-start | bytes 8388608 | tf_op jit(solution)/shard_map/all_to_all | solution.py:44
  79.5 0.0 copy-done.1
  79.5 0.1 copy.22
  79.6 0.7 select_reduce_fusion
  80.3 53.5 %all-to-all-done.1 = bf16[16,64,2048]{2,1,0:T(8,128)(2,1)} async-done(((bf16[16,64,2048]{2,1,0:T(8,128)(2,1)}), bf16[16,64,2048]{2,1,0:T(8,128)(2,1)}, u32[]{:S(2)}, u32[]{:S(2)}) %all-to-all-start.1) | async-done | bytes 4194336 | tf_op jit(solution)/shard_map/all_to_all | solution.py:44
  133.8 5.2 %convolution_convert_fusion.2 = bf16[64,2048]{1,0:T(8,128)(2,1)} fusion(f32[64,1024]{1,0:T(8,128)S(1)} %select_reduce_fusion, bf16[1024,2048]{1,0:T(8,128)(2,1)} %bitcast.5), kind=kOutput, calls=%fused_computation.7 | convolution fusion | flops 1610743808 | bytes 4718592 | tf_op jit(solution)/shard_map/dot_general | solution.py:48
  (2 shorter events, 0.0 us)
Async XLA Ops:
  0.0 69.7 %copy-start = (bf16[1,768,2048]{2,1,0:T(8,128)(2,1)S(1)}, bf16[1,768,2048]{2,1,0:T(8,128)(2,1)}, u32[]{:S(2)}) copy-start(bf16[1,768,2048]{2,1,0:T(8,128)(2,1)} %param.9) | copy-start | bytes 9437188
  2.9 60.1 %slice-start = ((s8[6291456]{0:T(1024)(128)(4,1)}), s8[4194304]{0:T(1024)(128)(4,1)S(1)}, s32[]{:S(2)}) async-start(s8[6291456]{0:T(1024)(128)(4,1)} %bitcast.18), calls=%async_computation.2 | async-start | bytes 8388608
  5.3 57.7 %slice-start.1 = ((s8[6291456]{0:T(1024)(128)(4,1)}), s8[2097152]{0:T(1024)(128)(4,1)S(1)}, s32[]{:S(2)}) async-start(s8[6291456]{0:T(1024)(128)(4,1)} %bitcast.18), calls=%async_computation.3 | async-start | bytes 4194304
  74.8 4.7 %copy-start.1 = (f32[64,8]{0,1:T(8,128)S(1)}, f32[64,8]{0,1:T(8,128)}, u32[]{:S(2)}) copy-start(f32[64,8]{0,1:T(8,128)} %param.7) | copy-start | bytes 6148
  74.8 59.0 %all-to-all-start.1 = ((bf16[16,64,2048]{2,1,0:T(8,128)(2,1)}), bf16[16,64,2048]{2,1,0:T(8,128)(2,1)}, u32[]{:S(2)}, u32[]{:S(2)}) async-start(bf16[16,64,2048]{2,1,0:T(8,128)(2,1)} %bitcast.16), calls=%async_computation.1 | async-start | bytes 8388608 | tf_op jit(solution)/shard_map/all_to_all | solution.py:44

commit v5 on v2

v5 whole, which is shorter than its diff:
```python
import jax
import jax.numpy as jnp
from jax import lax
from jax.sharding import Mesh
from jax.sharding import PartitionSpec as P

SIDE = 4
PAD = 128


def body(hidden_in, route_ids, gates, w_in, w_out):
    me = lax.axis_index("ex") * SIDE + lax.axis_index("ey")
    count, width = hidden_in.shape
    half = w_out.shape[1]
    experts = jnp.arange(SIDE * SIDE, dtype=jnp.int32)
    table = jnp.sum(
        jnp.where(route_ids[:, :, None] == experts, gates[:, :, None], jnp.float32(0.0)), axis=1
    )
    high = table.astype(jnp.bfloat16)
    low = (table - high.astype(jnp.float32)).astype(jnp.bfloat16)
    extra = jnp.zeros((count, PAD - 2 * SIDE * SIDE), jnp.bfloat16)
    payload = jnp.concatenate([hidden_in, high, low, extra], axis=1)
    stage = lax.all_gather(payload, "ey", axis=0, tiled=True)
    rows = lax.all_gather(stage, "ex", axis=0, tiled=True)
    picked = (experts == me)[None, :]
    got_high = rows[:, width:width + SIDE * SIDE].astype(jnp.float32)
    got_low = rows[:, width + SIDE * SIDE:width + 2 * SIDE * SIDE].astype(jnp.float32)
    mine = jnp.sum(jnp.where(picked, got_high + got_low, jnp.float32(0.0)), axis=1)
    projected = jnp.dot(rows[:, :width], w_in[0], preferred_element_type=jnp.float32)
    inner = (jax.nn.silu(projected[:, :half]) * projected[:, half:]).astype(jnp.bfloat16)
    produced = jnp.dot(inner, w_out[0], preferred_element_type=jnp.float32).astype(jnp.bfloat16)
    weighted = (mine[:, None] * produced.astype(jnp.float32)).astype(jnp.bfloat16)
    part = lax.psum_scatter(weighted, "ex", scatter_dimension=0, tiled=True)
    return lax.psum_scatter(part, "ey", scatter_dimension=0, tiled=True)


def solution(mesh):
    grid = Mesh(mesh.devices.reshape(mesh.shape["dp"], SIDE, SIDE), ("dp", "ex", "ey"))
    rows = P(("dp", "ex", "ey"), None)
    placed = (rows, rows, rows, P(("ex", "ey"), None, None), P(("ex", "ey"), None, None))
    return jax.shard_map(body, mesh=grid, in_specs=placed, out_specs=rows, check_vma=False)
```

time: 198 us -> 196 us (0.990)
  waiting for transfers between devices: 76.5 us -> 163 us
  blocking collectives: 39.5 us -> 0 us
  local copies, waits for them, and re-layouts: 31.4 us -> 1.94 us
  starting transfers between devices: 26 us -> 0.12 us
  between operations: 0.13 us -> 13.2 us
  other arithmetic: 10.7 us -> 2.33 us
  matrix products: 12.9 us -> 15.1 us
    all_gather x0 -> x2, waiting for transfers between devices: none -> 84.3 us  [the longest x1 55.1 us: body(): rows = lax.all_gather(stage, 'ex', axis=0, tiled=True)]
    reduce_scatter x0 -> x2, waiting for transfers between devices: none -> 78.4 us  [the longest x1 49.9 us: body(): part = lax.psum_scatter(weighted, 'ex', scatter_dimension=0, tiled=True)]
    all_to_all x6 -> x0, waiting for transfers between devices: 76.5 us -> none  [the longest x3 45.9 us: spread(): return lax.all_to_all(copies, axis, 0, 0, tiled=False)]
    all_to_all x2 -> x0, blocking collectives: 39.5 us -> none  [the longest x1 25.3 us: collect(): moved = lax.all_to_all(parts.astype(jnp.bfloat16), axis, 0, 0, tiled=False)]
    all_to_all x6 -> x0, starting transfers between devices: 26 us -> none  [the longest x3 13.2 us: spread(): return lax.all_to_all(copies, axis, 0, 0, tiled=False)]
    broadcast_in_dim x6 -> x0, local copies, waits for them, and re-layouts: 10.5 us -> none  [spread(): copies = jnp.broadcast_to(block[None], (SIDE,) + block.shape)]
    all_to_all x2 -> x0, local copies, waits for them, and re-layouts: 8.31 us -> none  [spread(): return lax.all_to_all(copies, axis, 0, 0, tiled=False)]
    reshape x2 -> x0, local copies, waits for them, and re-layouts: 8.22 us -> none  [body(): gathered.append(spread(stage, second).reshape(SIDE * SIDE * split, -1))]
  transfers between devices with their start and end apart: 6 -> 4, of which waited for: 6 -> 4; matrix products, arithmetic and copies ran while one was open for 10% -> 0% of each run, Pallas kernels for 0% -> 0%
where the time goes in v5:
time: 196 us; the launch traced here: 195 us
  waiting for transfers between devices  163 us (83%)
  matrix products  15.1 us (8%)
  between operations  13.2 us (7%)
  other arithmetic  2.33 us (1%)
    all_gather x1, waiting for transfers between devices, body(): rows = lax.all_gather(stage, 'ex', axis=0, tiled=True)  55.1 us
    reduce_scatter x1, waiting for transfers between devices, body(): part = lax.psum_scatter(weighted, 'ex', scatter_dimension=0, tiled=True)  49.9 us
    all_gather x1, waiting for transfers between devices, body(): stage = lax.all_gather(payload, 'ey', axis=0, tiled=True)  29.2 us
    reduce_scatter x1, waiting for transfers between devices, body(): return lax.psum_scatter(part, 'ey', scatter_dimension=0, tiled=True)  28.5 us
    dot_general x1, matrix products, body(): jnp.dot(rows[:, :width], w_in[0], preferred_element_type=jnp.float32)  10 us
    dot_general x1, matrix products, body(): jnp.dot(inner, w_out[0], preferred_element_type=jnp.float32)  5.09 us
  transfers between devices with their start and end apart: 4, of which 4 were waited for; matrix products, arithmetic and copies ran while one was open for 0% of the time, Pallas kernels for 0%

profile of v5, /device:TPU:64, one launch (start us, length us, event | category | flops | bytes accessed | tf_op | source)
XLA Modules:
  0.0 195.4 jit_solution(14365976159302029597)
XLA Ops:
  6.5 0.0 copy-start
  6.5 0.0 all-gather.3.cloned.1.call-start
  6.5 0.9 select_reduce_fusion.1
  7.4 0.1 copy.9
  7.5 0.1 copy.8
  7.6 1.7 concatenate.3
  9.4 0.0 all-gather.3.cloned.1.call-update
  9.4 0.0 all-gather.5.cloned.1.call-start
  9.4 29.2 %all-gather.3.cloned.1.call-done = bf16[256,2176]{1,0:T(8,128)(2,1)} async-done(((bf16[64,2176]{1,0:T(8,128)(2,1)}), bf16[256,2176]{1,0:T(8,128)(2,1)}) %all-gather.3.cloned.1.call-update) | async-done | bytes 1114128 | tf_op jit(solution)/shard_map/all_gather | solution.py:23
  38.6 0.0 all-gather.5.cloned.1.call-update
  38.6 0.0 reduce-scatter.3.cloned.1.call-start
  38.7 55.1 %all-gather.5.cloned.1.call-done = bf16[1024,2176]{1,0:T(8,128)(2,1)} async-done(((bf16[256,2176]{1,0:T(8,128)(2,1)}), bf16[1024,2176]{1,0:T(8,128)(2,1)}) %all-gather.5.cloned.1.call-update) | async-done | bytes 4456464 | tf_op jit(solution)/shard_map/all_gather | solution.py:24
  93.8 1.4 select_reduce_fusion
  95.3 10.0 %fusion = f32[1024,1536]{1,0:T(8,128)S(1)} fusion(bf16[1,2048,1536]{2,1,0:T(8,128)(2,1)} %param.8, bf16[1024,2176]{1,0:T(8,128)(2,1)} %all-gather.5.cloned.1.call-done), kind=kOutput, calls=%fused_computation.1 | convolution fusion | flops 6442450944 | bytes 16777216 | tf_op jit(solution)/shard_map/dot_general | solution.py:29
  105.3 0.0 copy-done
  105.3 5.1 %multiply_convert_fusion = bf16[1024,2048]{1,0:T(8,128)(2,1)} fusion(f32[1024]{0:T(1024)S(1)} %select_reduce_fusion, bf16[1,768,2048]{2,1,0:T(8,128)(2,1)S(1)} %copy-done, f32[1024,1536]{1,0:T(8,128)S(1)} %fusion), kind=kOutput, calls=%fused_computation | convolution fusion | flops 3234332672 | bytes 13635584 | tf_op jit(solution)/shard_map/dot_general | solution.py:31
  110.4 0.0 reduce-scatter.3.cloned.1.call-update
  110.4 0.0 reduce-scatter.5.cloned.1.call-start
  110.5 49.9 %reduce-scatter.3.cloned.1.call-done = bf16[256,2048]{1,0:T(8,128)(2,1)} async-done(((bf16[1024,2048]{1,0:T(8,128)(2,1)}), bf16[256,2048]{1,0:T(8,128)(2,1)}) %reduce-scatter.3.cloned.1.call-update) | async-done | bytes 1048592 | tf_op jit(solution)/shard_map/reduce_scatter | solution.py:33
  160.4 0.0 reduce-scatter.5.cloned.1.call-update
  160.4 28.5 %reduce-scatter.5.cloned.1.call-done = bf16[64,2048]{1,0:T(8,128)(2,1)} async-done(((bf16[256,2048]{1,0:T(8,128)(2,1)}), bf16[64,2048]{1,0:T(8,128)(2,1)}) %reduce-scatter.5.cloned.1.call-update) | async-done | bytes 262160 | tf_op jit(solution)/shard_map/reduce_scatter | solution.py:34
  (3 shorter events, 0.0 us)
Async XLA Ops:
  6.5 98.8 %copy-start = (bf16[1,768,2048]{2,1,0:T(8,128)(2,1)S(1)}, bf16[1,768,2048]{2,1,0:T(8,128)(2,1)}, u32[]{:S(2)}) copy-start(bf16[1,768,2048]{2,1,0:T(8,128)(2,1)} %param.9) | copy-start | bytes 9437188
  6.5 32.1 %all-gather.3.cloned.1.call-start = ((), (), s32[]{:S(2)}) async-start(), calls=%async_computation.2 | async-start | bytes 1392640 | tf_op jit(solution)/shard_map/all_gather | solution.py:23
  9.4 84.4 %all-gather.5.cloned.1.call-start = ((), (), s32[]{:S(2)}) async-start(), calls=%async_computation.3 | async-start | bytes 5570560 | tf_op jit(solution)/shard_map/all_gather | solution.py:24
  38.6 121.7 %reduce-scatter.3.cloned.1.call-start = ((), (), s32[]{:S(2)}) async-start(), calls=%async_computation.4 | async-start | bytes 5242880 | tf_op jit(solution)/shard_map/reduce_scatter | solution.py:33
  110.4 78.5 %reduce-scatter.5.cloned.1.call-start = ((), (), s32[]{:S(2)}) async-start(), calls=%async_computation.5 | async-start | bytes 1310720 | tf_op jit(solution)/shard_map/reduce_scatter | solution.py:34
Sparse Core Ops, SparseCore 0:
  9.5 29.0 all-gather.2
  40.4 53.3 all-gather.4
  110.5 49.7 reduce-scatter.2
  162.8 26.0 reduce-scatter.4
